TPU v7x, 32 devices: a whole 2x2x4 slice. The times are simulated.
32 devices in a mesh: grp: 8 (over z, x), rep: 4 (over y, core).
Axes of the slice: x: 2, y: 2, z: 4, core: 2. Of those that a mesh axis runs over, the one named last changes fastest.
Arguments:
- three_center: bfloat16 [4, 64, 32, 6, 4096], P('rep', 'grp'), may hold values from -2 to 2
- metric: bfloat16 [4, 64, 64], P('rep'), may hold values from -0.75 to 0.75
- occupied: bfloat16 [2048, 48], replicated, may hold values from -0.3125 to 0.3125
- nu_list: int32 [32, 6], replicated, may hold values from 0 to 31, as said below
- nu_count: int32 [32], replicated, may hold values from 1 to 6
- block_size: int32 [32], replicated, may hold values from 32 to 64
Outputs:
- exchange_matrix: float32 [2048, 2048], P('rep', 'grp')
Inputs may be any that keep to these rules, and one draw needn't show every extreme that they name: `nu_list`: entry 0 of row m is m itself; the other entries of a row are distinct blocks other than m.
All inputs are finite; a program needn't handle non-finite values.
Results may differ from a plain program's by a relative error of at most 0.0024.
Values may be sent and summed in bfloat16 or wider, within the bound.
No kernel may reach another device: no remote copies, remote signals or barrier semaphores. Data moves between devices by JAX's collectives and lax.ppermute only.
A program may use at most 192 MiB of HBM per device.

v0:
```python
import jax
import jax.numpy as jnp
from jax import lax
from jax.sharding import PartitionSpec as P

NB = 64
N_CHUNKS = 4


def body(three_center, metric, occupied, nu_list, nu_count, block_size):
    n_mu, knu = nu_list.shape
    n_occ = occupied.shape[1]
    aux_dev = three_center.shape[1]
    occ_c = n_occ // N_CHUNKS
    lanes = jnp.arange(NB, dtype=jnp.int32)
    row_live = lanes[None, :] < block_size[:, None]
    col_live = lanes[None, None, :] < block_size[nu_list][:, :, None]
    slot_live = jnp.arange(knu, dtype=jnp.int32)[None, :] < nu_count[:, None]
    mask = row_live[:, None, :, None] & col_live[:, :, None, :] & slot_live[:, :, None, None]
    blocks = three_center[0].reshape(aux_dev, n_mu, knu, NB, NB)
    masked = jnp.where(mask[None], blocks, jnp.zeros((), jnp.bfloat16))
    picked = occupied.reshape(n_mu, NB, N_CHUNKS, occ_c)[nu_list]
    half = jnp.einsum(
        "qmkab,mkbci->cqmai", masked, picked, preferred_element_type=jnp.float32
    ).astype(jnp.bfloat16)
    half = half.reshape(N_CHUNKS, aux_dev, n_mu, NB * occ_c)
    n_grp = lax.axis_size("grp")
    rows = n_mu * NB // n_grp
    start = lax.axis_index("grp") * rows
    term = None
    for c in range(N_CHUNKS):
        gathered = lax.all_gather(half[c], "grp", axis=0, tiled=True)
        n_aux = gathered.shape[0]
        gathered = gathered.reshape(n_aux, n_mu, NB, occ_c)
        orbital = jnp.einsum(
            "pq,qmai->mapi", metric[0], gathered, preferred_element_type=jnp.float32
        ).astype(jnp.bfloat16)
        orbital = orbital.reshape(n_mu * NB, n_aux * occ_c)
        mine = lax.dynamic_slice_in_dim(orbital, start, rows, axis=0)
        part = jnp.dot(orbital, mine.T, preferred_element_type=jnp.float32)
        term = part if term is None else term + part
    return lax.psum_scatter(term, "rep", scatter_dimension=0, tiled=True)


def solution(mesh):
    return jax.shard_map(
        body,
        mesh=mesh,
        in_specs=(P("rep", "grp", None, None, None), P("rep", None, None), P(), P(), P(), P()),
        out_specs=P("rep", "grp"),
        check_vma=False,
    )
```

profile of v0, /device:TPU:0, one launch (start us, length us, event | category | flops | bytes accessed | tf_op | source)
XLA Modules:
  0.0 872.6 jit_solution(10821817166071291102)
XLA Ops:
  6.6 34.4 %reshape_squeeze.3 = bf16[8,32,6,64,64]{4,3,1,2,0:T(8,128)(2,1)} reshape(bf16[1,8,32,6,4096]{4,2,3,1,0:T(8,128)(2,1)} %param.6) | data formatting | bytes 25165824 | tf_op jit(solution)/shard_map/reshape;squeeze | solution.py:20
  41.0 0.1 iota_compare_fusion.1
  41.1 0.1 copy.27
  41.2 0.1 reshape.94
  41.3 0.1 iota_compare_fusion.2
  41.4 1.6 gather_fusion.1
  42.9 0.1 reshape.101
  43.0 0.1 iota_compare_fusion
  43.2 0.4 reshape.83
  43.5 0.3 copy.28
  43.9 2.6 gather_fusion
  46.5 1.6 and_and_fusion
  48.1 17.4 %fusion.4 = bf16[4,8,32,64,12]{3,4,1,0,2:T(8,128)(2,1)} fusion(bf16[8,32,6,64,64]{4,3,1,2,0:T(8,128)(2,1)} %reshape_squeeze.3, pred[32,6,64,64]{3,2,1,0:T(8,128)(4,1)S(1)} %and_and_fusion, bf16[32,6,64,4,12,1]{2,3,4,1,0,5:T(4,128)(2,1)S(1)} %bitcast.76), kind=kOutput, calls=%fused_computation.13 | convolution fusion | flops 611057664 | bytes 16121856 | tf_op jit(solution)/shard_map/qmkab,mkbci->cqmai/dot_general | solution.py:23
  65.4 4.3 fusion.22
  69.8 5.3 copy.31
  75.1 0.0 all-gather.7.cloned.1.call-start
  75.1 4.1 copy.35
  79.2 10.4 %all-gather.9.cloned.1.call-start = ((), (), s32[]{:S(2)}) async-start(), calls=%async_computation.3 | async-start | bytes 14155776 | tf_op jit(solution)/shard_map/all_gather | solution.py:32
  89.7 4.1 copy.39
  93.8 0.0 all-gather.11.cloned.1.call-start
  93.9 4.1 copy.43
  98.1 156.4 %all-gather.5.cloned.1.call-done = bf16[64,32,768]{1,0,2:T(8,128)(2,1)} async-done(((bf16[8,32,768]{1,0,2:T(8,128)(2,1)}), bf16[64,32,768]{1,0,2:T(8,128)(2,1)}) %all-gather.5.cloned.1.call-update) | async-done | bytes 3145744 | tf_op jit(solution)/shard_map/all_gather | solution.py:32
  254.5 15.7 %copy.33 = bf16[64,32,64,12]{0,2,3,1:T(8,128)(2,1)} copy(bf16[64,32,64,12]{1,0,3,2:T(8,128)(2,1)} %bitcast.77) | data formatting | bytes 6291456 | tf_op jit(solution)/shard_map/reshape | solution.py:34
  270.3 7.2 convert_bitcast_fusion.3
  277.5 9.4 %copy.34 = bf16[32,64,64,12]{1,0,3,2:T(8,128)(2,1)} copy(bf16[32,64,64,12]{2,1,3,0:T(8,128)(2,1)} %convert_bitcast_fusion.3) | data formatting | bytes 6291456 | tf_op jit(solution)/shard_map/convert_element_type | solution.py:37
  286.9 9.7 %reshape.85 = bf16[2048,768]{0,1:T(8,128)(2,1)} reshape(bf16[32,64,64,12]{1,0,3,2:T(8,128)(2,1)} %copy.34) | data formatting | bytes 6291456 | tf_op jit(solution)/shard_map/reshape | solution.py:38
  296.6 134.7 %all-gather.7.cloned.1.call-done = bf16[64,32,768]{1,0,2:T(8,128)(2,1)} async-done(((bf16[8,32,768]{1,0,2:T(8,128)(2,1)}), bf16[64,32,768]{1,0,2:T(8,128)(2,1)}) %all-gather.7.cloned.1.call-update) | async-done | bytes 3145744 | tf_op jit(solution)/shard_map/all_gather | solution.py:32
  431.4 15.8 %copy.37 = bf16[64,32,64,12]{0,2,3,1:T(8,128)(2,1)} copy(bf16[64,32,64,12]{1,0,3,2:T(8,128)(2,1)} %bitcast.78) | data formatting | bytes 6291456 | tf_op jit(solution)/shard_map/reshape | solution.py:34
  447.1 7.3 convert_bitcast_fusion.2
  454.4 9.4 %copy.38 = bf16[32,64,64,12]{1,0,3,2:T(8,128)(2,1)} copy(bf16[32,64,64,12]{2,1,3,0:T(8,128)(2,1)} %convert_bitcast_fusion.2) | data formatting | bytes 6291456 | tf_op jit(solution)/shard_map/convert_element_type | solution.py:37
  463.8 8.5 reshape.87
  472.3 135.9 %all-gather.9.cloned.1.call-done = bf16[64,32,768]{1,0,2:T(8,128)(2,1)} async-done(((bf16[8,32,768]{1,0,2:T(8,128)(2,1)}), bf16[64,32,768]{1,0,2:T(8,128)(2,1)}) %all-gather.9.cloned.1.call-update) | async-done | bytes 3145744 | tf_op jit(solution)/shard_map/all_gather | solution.py:32
  608.2 15.8 %copy.41 = bf16[64,32,64,12]{0,2,3,1:T(8,128)(2,1)} copy(bf16[64,32,64,12]{1,0,3,2:T(8,128)(2,1)} %bitcast.79) | data formatting | bytes 6291456 | tf_op jit(solution)/shard_map/reshape | solution.py:34
  624.0 7.2 convert_bitcast_fusion.1
  631.1 9.5 %copy.42 = bf16[32,64,64,12]{1,0,3,2:T(8,128)(2,1)} copy(bf16[32,64,64,12]{2,1,3,0:T(8,128)(2,1)} %convert_bitcast_fusion.1) | data formatting | bytes 6291456 | tf_op jit(solution)/shard_map/convert_element_type | solution.py:37
  640.6 9.7 %reshape.89 = bf16[2048,768]{0,1:T(8,128)(2,1)} reshape(bf16[32,64,64,12]{1,0,3,2:T(8,128)(2,1)} %copy.42) | data formatting | bytes 6291456 | tf_op jit(solution)/shard_map/reshape | solution.py:38
  650.4 134.5 %all-gather.11.cloned.1.call-done = bf16[64,32,768]{1,0,2:T(8,128)(2,1)} async-done(((bf16[8,32,768]{1,0,2:T(8,128)(2,1)}), bf16[64,32,768]{1,0,2:T(8,128)(2,1)}) %all-gather.11.cloned.1.call-update) | async-done | bytes 3145744 | tf_op jit(solution)/shard_map/all_gather | solution.py:32
  784.9 15.5 %copy.45 = bf16[64,32,64,12]{0,2,3,1:T(8,128)(2,1)} copy(bf16[64,32,64,12]{1,0,3,2:T(8,128)(2,1)} %bitcast.80) | data formatting | bytes 6291456 | tf_op jit(solution)/shard_map/reshape | solution.py:34
  800.3 7.2 convert_bitcast_fusion
  807.6 9.4 %copy.46 = bf16[32,64,64,12]{1,0,3,2:T(8,128)(2,1)} copy(bf16[32,64,64,12]{2,1,3,0:T(8,128)(2,1)} %convert_bitcast_fusion) | data formatting | bytes 6291456 | tf_op jit(solution)/shard_map/convert_element_type | solution.py:37
  817.0 9.7 %reshape.91 = bf16[2048,768]{0,1:T(8,128)(2,1)} reshape(bf16[32,64,64,12]{1,0,3,2:T(8,128)(2,1)} %copy.46) | data formatting | bytes 6291456 | tf_op jit(solution)/shard_map/reshape | solution.py:38
  826.7 3.0 fusion.11
  829.7 1.1 convolution_add_fusion.2
  830.8 0.8 copy-done.2
  831.6 1.0 convolution_add_fusion.1
  832.6 0.8 copy-done.3
  833.5 2.5 convolution_add_fusion
  836.0 29.8 %reduce-scatter.2.cloned.1.call-done = f32[512,256]{1,0:T(8,128)} async-done(((f32[2048,256]{1,0:T(8,128)}), f32[512,256]{1,0:T(8,128)}) %reduce-scatter.2.cloned.1.call-update) | async-done | bytes 524304 | tf_op jit(solution)/shard_map/reduce_scatter | solution.py:42
  (21 shorter events, 0.2 us)
Async XLA Ops:
  6.5 263.7 %copy-start = (bf16[1,64,64]{2,1,0:T(8,128)(2,1)S(1)}, bf16[1,64,64]{2,1,0:T(8,128)(2,1)}, u32[]{:S(2)}) copy-start(bf16[1,64,64]{2,1,0:T(8,128)(2,1)} %param.7) | copy-start | bytes 24580
  6.5 34.5 %copy-start.6 = (s32[32]{0:T(128)S(1)}, s32[32]{0:T(128)}, u32[]{:S(2)}) copy-start(s32[32]{0:T(128)} %param.10) | copy-start | bytes 388
  6.5 34.5 %copy-start.5 = (s32[32,6]{0,1:T(8,128)S(1)}, s32[32,6]{0,1:T(8,128)}, u32[]{:S(2)}) copy-start(s32[32,6]{0,1:T(8,128)} %param.9) | copy-start | bytes 2308
  6.5 34.8 %copy-start.1 = (s32[32]{0:T(128)S(1)}, s32[32]{0:T(128)}, u32[]{:S(2)}) copy-start(s32[32]{0:T(128)} %param.11) | copy-start | bytes 388
  6.5 248.0 %all-gather.5.cloned.1.call-start = ((), (), s32[]{:S(2)}) async-start(), calls=%async_computation.1 | async-start | bytes 14155776 | tf_op jit(solution)/shard_map/all_gather | solution.py:32
  41.4 1.8 copy-start.4
  75.1 356.3 %all-gather.7.cloned.1.call-start = ((), (), s32[]{:S(2)}) async-start(), calls=%async_computation.2 | async-start | bytes 14155776 | tf_op jit(solution)/shard_map/all_gather | solution.py:32
  79.2 528.9 %all-gather.9.cloned.1.call-start = ((), (), s32[]{:S(2)}) async-start(), calls=%async_computation.3 | async-start | bytes 14155776 | tf_op jit(solution)/shard_map/all_gather | solution.py:32
  93.8 691.1 %all-gather.11.cloned.1.call-start = ((), (), s32[]{:S(2)}) async-start(), calls=%async_computation.4 | async-start | bytes 14155776 | tf_op jit(solution)/shard_map/all_gather | solution.py:32
  98.0 767.7 %reduce-scatter.2.cloned.1.call-start = ((), (), s32[]{:S(2)}) async-start(), calls=%async_computation.5 | async-start | bytes 2621440 | tf_op jit(solution)/shard_map/reduce_scatter | solution.py:42
  829.7 1.9 copy-start.2
  831.6 1.9 copy-start.3
Sparse Core Ops, SparseCore 0:
  75.2 179.2 all-gather.4
  256.6 174.7 all-gather.6
  433.4 174.7 all-gather.8
  610.1 174.7 all-gather.10
  836.1 29.6 reduce-scatter.1
where the time goes:
time: 885 us; the launch traced here: 873 us
  waiting for transfers between devices  591 us (67%)
  local copies, waits for them, and re-layouts  201 us (23%)
  matrix products  53.9 us (6%)
  between operations  13.7 us (2%)
  starting transfers between devices  10.6 us (1%)
    all_gather x4, waiting for transfers between devices, body(): gathered = lax.all_gather(half[c], 'grp', axis=0, tiled=True)  562 us
    reshape x4, local copies, waits for them, and re-layouts, body(): gathered = gathered.reshape(n_aux, n_mu, NB, occ_c)  62.7 us
    reshape x4, local copies, waits for them, and re-layouts, body(): orbital = orbital.reshape(n_mu * NB, n_aux * occ_c)  37.7 us
    convert_element_type x4, local copies, waits for them, and re-layouts, body(): orbital = jnp.einsum('pq,qmai->mapi', metric[0], gathered, preferred_elem...  37.7 us
    another operation x1, local copies, waits for them, and re-layouts, body(): blocks = three_center[0].reshape(aux_dev, n_mu, knu, NB, NB)  34.4 us
    reduce_scatter x1, waiting for transfers between devices, body(): return lax.psum_scatter(term, 'rep', scatter_dimension=0, tiled=True)  29.8 us
    dot_general x4, matrix products, body(): jnp.einsum('pq,qmai->mapi', metric[0], gathered, preferred_element_type=j...  28.9 us
    slice x5, local copies, waits for them, and re-layouts, body(): gathered = lax.all_gather(half[c], 'grp', axis=0, tiled=True)  22 us
  transfers between devices with their start and end apart: 5, of which 5 were waited for; matrix products, arithmetic and copies ran while one was open for 16% of the time, Pallas kernels for 0%

commit v1 on v0

--- a/solution.py
+++ b/solution.py
@@ -29,7 +29,14 @@
     start = lax.axis_index("grp") * rows
     term = None
     for c in range(N_CHUNKS):
-        gathered = lax.all_gather(half[c], "grp", axis=0, tiled=True)
+        ring = [half[c]]
+        for hop in range(7):
+            ring.append(lax.ppermute(ring[-1], "grp", [(dev, (dev + 1) % 8) for dev in range(8)]))
+        gathered = jnp.roll(
+            jnp.concatenate(ring[::-1], axis=0),
+            (lax.axis_index("grp") + 1) * ring[0].shape[0],
+            axis=0,
+        )
         n_aux = gathered.shape[0]
         gathered = gathered.reshape(n_aux, n_mu, NB, occ_c)
         orbital = jnp.einsum(

time: 885 us -> 573 us (0.65)
  waiting for transfers between devices: 591 us -> 239 us
  matrix products: 53.9 us -> 76.4 us
  other arithmetic: 1.82 us -> 13.4 us
    all_gather x4 -> x0, waiting for transfers between devices: 562 us -> none  [body(): gathered = lax.all_gather(half[c], 'grp', axis=0, tiled=True)]
    ppermute x0 -> x28, waiting for transfers between devices: none -> 209 us  [body(): lax.ppermute(ring[-1], 'grp', [(dev, (dev + 1) % 8) for dev in range(8)])]
    reshape x4 -> x0, local copies, waits for them, and re-layouts: 62.7 us -> none  [body(): gathered = gathered.reshape(n_aux, n_mu, NB, occ_c)]
    unnamed x14 -> x78, local copies, waits for them, and re-layouts: 1.61 us -> 62.8 us
    dot_general x4, matrix products: 28.9 us -> 51.2 us  [body(): jnp.einsum('pq,qmai->mapi', metric[0], gathered, preferred_element_type=j...]
    ppermute x0 -> x28, starting transfers between devices: none -> 11.2 us  [body(): lax.ppermute(ring[-1], 'grp', [(dev, (dev + 1) % 8) for dev in range(8)])]
    all_gather x4 -> x0, starting transfers between devices: 10.5 us -> none  [body(): gathered = lax.all_gather(half[c], 'grp', axis=0, tiled=True)]
    concatenate x0 -> x2, other arithmetic: none -> 9.54 us  [body(): jnp.roll(jnp.concatenate(ring[::-1], axis=0), (lax.axis_index('grp') + 1)...]
  transfers between devices with their start and end apart: 5 -> 29, of which waited for: 5 -> 25; matrix products, arithmetic and copies ran while one was open for 16% -> 5% of each run, Pallas kernels for 0% -> 0%
where the time goes in v1:
time: 573 us; the launch traced here: 562 us
  waiting for transfers between devices  239 us (42%)
  local copies, waits for them, and re-layouts  207 us (36%)
  matrix products  76.4 us (13%)
  between operations  14.3 us (2%)
  other arithmetic  13.4 us (2%)
  starting transfers between devices  11.2 us (2%)
    ppermute x28, waiting for transfers between devices, body(): lax.ppermute(ring[-1], 'grp', [(dev, (dev + 1) % 8) for dev in range(8)])  209 us
    unnamed x78, local copies, waits for them, and re-layouts  62.8 us
    dot_general x4, matrix products, body(): jnp.einsum('pq,qmai->mapi', metric[0], gathered, preferred_element_type=j...  51.2 us
    reshape x4, local copies, waits for them, and re-layouts, body(): orbital = orbital.reshape(n_mu * NB, n_aux * occ_c)  38.2 us
    convert_element_type x4, local copies, waits for them, and re-layouts, body(): orbital = jnp.einsum('pq,qmai->mapi', metric[0], gathered, preferred_elem...  38.1 us
    another operation x1, local copies, waits for them, and re-layouts, body(): blocks = three_center[0].reshape(aux_dev, n_mu, knu, NB, NB)  34.4 us
    reduce_scatter x1, waiting for transfers between devices, body(): return lax.psum_scatter(term, 'rep', scatter_dimension=0, tiled=True)  30.1 us
    slice x5, local copies, waits for them, and re-layouts, body(): ring = [half[c]]  23.2 us
  transfers between devices with their start and end apart: 29, of which 25 were waited for; matrix products, arithmetic and copies ran while one was open for 5% of the time, Pallas kernels for 0%

profile of v1, /device:TPU:0, one launch (start us, length us, event | category | flops | bytes accessed | tf_op | source)
XLA Modules:
  0.0 561.7 jit_solution(14481433671691483533)
XLA Ops:
  14.1 34.4 %reshape_squeeze.3 = bf16[8,32,6,64,64]{4,3,1,2,0:T(8,128)(2,1)} reshape(bf16[1,8,32,6,4096]{4,2,3,1,0:T(8,128)(2,1)} %param.8) | data formatting | bytes 25165824 | tf_op jit(solution)/shard_map/reshape;squeeze | solution.py:20
  50.0 17.4 %fusion.12 = bf16[4,8,32,64,12]{3,4,1,0,2:T(8,128)(2,1)} fusion(bf16[8,32,6,64,64]{4,3,1,2,0:T(8,128)(2,1)} %reshape_squeeze.3, pred[32,6,64,64]{3,2,1,0:T(8,128)(4,1)S(1)} %and_and_fusion, bf16[32,6,64,4,12,1]{2,3,4,1,0,5:T(4,128)(2,1)S(1)} %bitcast.72), kind=kOutput, calls=%fused_computation.29 | convolution fusion | flops 611057664 | bytes 16121856 | tf_op jit(solution)/shard_map/qmkab,mkbci->cqmai/dot_general | solution.py:23
  67.4 4.7 fusion.42
  72.0 4.9 copy.51
  81.9 4.9 copy.69
  89.5 4.9 copy.63
  106.3 5.8 %collective-permute-done.14 = bf16[8,32,768]{2,1,0:T(8,128)(2,1)} collective-permute-done((bf16[8,32,768]{2,1,0:T(8,128)(2,1)S(1)}, bf16[8,32,768]{2,1,0:T(8,128)(2,1)}, u32[]{:S(2)}, u32[]{:S(2)}) %collective-permute-start.14) | collective-permute-done | bytes 393248 | tf_op jit(solution)/shard_map/ppermute | solution.py:34
  112.1 8.3 %collective-permute-done.7 = bf16[8,32,768]{2,1,0:T(8,128)(2,1)S(1)} collective-permute-done((bf16[8,32,768]{2,1,0:T(8,128)(2,1)S(1)}, bf16[8,32,768]{2,1,0:T(8,128)(2,1)S(1)}, u32[]{:S(2)}, u32[]{:S(2)}) %collective-permute-start.7) | collective-permute-done | bytes 393248 | tf_op jit(solution)/shard_map/ppermute | solution.py:34
  120.4 8.4 %collective-permute-done.1 = bf16[8,32,768]{2,1,0:T(8,128)(2,1)S(1)} collective-permute-done((bf16[8,32,768]{2,1,0:T(8,128)(2,1)}, bf16[8,32,768]{2,1,0:T(8,128)(2,1)S(1)}, u32[]{:S(2)}, u32[]{:S(2)}) %collective-permute-start.1) | collective-permute-done | bytes 393248 | tf_op jit(solution)/shard_map/ppermute | solution.py:34
  128.9 8.4 %collective-permute-done.22 = bf16[8,32,768]{2,1,0:T(8,128)(2,1)S(1)} collective-permute-done((bf16[8,32,768]{2,1,0:T(8,128)(2,1)}, bf16[8,32,768]{2,1,0:T(8,128)(2,1)S(1)}, u32[]{:S(2)}, u32[]{:S(2)}) %collective-permute-start.22) | collective-permute-done | bytes 393248 | tf_op jit(solution)/shard_map/ppermute | solution.py:34
  137.3 8.4 %collective-permute-done.15 = bf16[8,32,768]{2,1,0:T(8,128)(2,1)S(1)} collective-permute-done((bf16[8,32,768]{2,1,0:T(8,128)(2,1)}, bf16[8,32,768]{2,1,0:T(8,128)(2,1)S(1)}, u32[]{:S(2)}, u32[]{:S(2)}) %collective-permute-start.15) | collective-permute-done | bytes 393248 | tf_op jit(solution)/shard_map/ppermute | solution.py:34
  145.7 8.4 %collective-permute-done.8 = bf16[8,32,768]{2,1,0:T(8,128)(2,1)S(1)} collective-permute-done((bf16[8,32,768]{2,1,0:T(8,128)(2,1)S(1)}, bf16[8,32,768]{2,1,0:T(8,128)(2,1)S(1)}, u32[]{:S(2)}, u32[]{:S(2)}) %collective-permute-start.8) | collective-permute-done | bytes 393248 | tf_op jit(solution)/shard_map/ppermute | solution.py:34
  154.1 8.4 %collective-permute-done.2 = bf16[8,32,768]{2,1,0:T(8,128)(2,1)S(1)} collective-permute-done((bf16[8,32,768]{2,1,0:T(8,128)(2,1)S(1)}, bf16[8,32,768]{2,1,0:T(8,128)(2,1)S(1)}, u32[]{:S(2)}, u32[]{:S(2)}) %collective-permute-start.2) | collective-permute-done | bytes 393248 | tf_op jit(solution)/shard_map/ppermute | solution.py:34
  162.6 8.4 %collective-permute-done.23 = bf16[8,32,768]{2,1,0:T(8,128)(2,1)S(1)} collective-permute-done((bf16[8,32,768]{2,1,0:T(8,128)(2,1)S(1)}, bf16[8,32,768]{2,1,0:T(8,128)(2,1)S(1)}, u32[]{:S(2)}, u32[]{:S(2)}) %collective-permute-start.23) | collective-permute-done | bytes 393248 | tf_op jit(solution)/shard_map/ppermute | solution.py:34
  171.0 8.4 %collective-permute-done.16 = bf16[8,32,768]{2,1,0:T(8,128)(2,1)S(1)} collective-permute-done((bf16[8,32,768]{2,1,0:T(8,128)(2,1)S(1)}, bf16[8,32,768]{2,1,0:T(8,128)(2,1)S(1)}, u32[]{:S(2)}, u32[]{:S(2)}) %collective-permute-start.16) | collective-permute-done | bytes 393248 | tf_op jit(solution)/shard_map/ppermute | solution.py:34
  179.4 8.4 %collective-permute-done.9 = bf16[8,32,768]{2,1,0:T(8,128)(2,1)S(1)} collective-permute-done((bf16[8,32,768]{2,1,0:T(8,128)(2,1)S(1)}, bf16[8,32,768]{2,1,0:T(8,128)(2,1)S(1)}, u32[]{:S(2)}, u32[]{:S(2)}) %collective-permute-start.9) | collective-permute-done | bytes 393248 | tf_op jit(solution)/shard_map/ppermute | solution.py:34
  187.8 8.4 %collective-permute-done.3 = bf16[8,32,768]{2,1,0:T(8,128)(2,1)S(1)} collective-permute-done((bf16[8,32,768]{2,1,0:T(8,128)(2,1)S(1)}, bf16[8,32,768]{2,1,0:T(8,128)(2,1)S(1)}, u32[]{:S(2)}, u32[]{:S(2)}) %collective-permute-start.3) | collective-permute-done | bytes 393248 | tf_op jit(solution)/shard_map/ppermute | solution.py:34
  196.3 8.4 %collective-permute-done.24 = bf16[8,32,768]{2,1,0:T(8,128)(2,1)S(1)} collective-permute-done((bf16[8,32,768]{2,1,0:T(8,128)(2,1)S(1)}, bf16[8,32,768]{2,1,0:T(8,128)(2,1)S(1)}, u32[]{:S(2)}, u32[]{:S(2)}) %collective-permute-start.24) | collective-permute-done | bytes 393248 | tf_op jit(solution)/shard_map/ppermute | solution.py:34
  204.7 8.4 %collective-permute-done.17 = bf16[8,32,768]{2,1,0:T(8,128)(2,1)S(1)} collective-permute-done((bf16[8,32,768]{2,1,0:T(8,128)(2,1)S(1)}, bf16[8,32,768]{2,1,0:T(8,128)(2,1)S(1)}, u32[]{:S(2)}, u32[]{:S(2)}) %collective-permute-start.17) | collective-permute-done | bytes 393248 | tf_op jit(solution)/shard_map/ppermute | solution.py:34
  213.1 8.4 %collective-permute-done.10 = bf16[8,32,768]{2,1,0:T(8,128)(2,1)S(1)} collective-permute-done((bf16[8,32,768]{2,1,0:T(8,128)(2,1)S(1)}, bf16[8,32,768]{2,1,0:T(8,128)(2,1)S(1)}, u32[]{:S(2)}, u32[]{:S(2)}) %collective-permute-start.10) | collective-permute-done | bytes 393248 | tf_op jit(solution)/shard_map/ppermute | solution.py:34
  221.5 8.4 %collective-permute-done.4 = bf16[8,32,768]{2,1,0:T(8,128)(2,1)S(1)} collective-permute-done((bf16[8,32,768]{2,1,0:T(8,128)(2,1)S(1)}, bf16[8,32,768]{2,1,0:T(8,128)(2,1)S(1)}, u32[]{:S(2)}, u32[]{:S(2)}) %collective-permute-start.4) | collective-permute-done | bytes 393248 | tf_op jit(solution)/shard_map/ppermute | solution.py:34
  230.0 8.5 %collective-permute-done.25 = bf16[8,32,768]{2,1,0:T(8,128)(2,1)} collective-permute-done((bf16[8,32,768]{2,1,0:T(8,128)(2,1)S(1)}, bf16[8,32,768]{2,1,0:T(8,128)(2,1)}, u32[]{:S(2)}, u32[]{:S(2)}) %collective-permute-start.25) | collective-permute-done | bytes 393248 | tf_op jit(solution)/shard_map/ppermute | solution.py:34
  238.5 8.4 %collective-permute-done.18 = bf16[8,32,768]{2,1,0:T(8,128)(2,1)} collective-permute-done((bf16[8,32,768]{2,1,0:T(8,128)(2,1)S(1)}, bf16[8,32,768]{2,1,0:T(8,128)(2,1)}, u32[]{:S(2)}, u32[]{:S(2)}) %collective-permute-start.18) | collective-permute-done | bytes 393248 | tf_op jit(solution)/shard_map/ppermute | solution.py:34
  246.9 8.4 %collective-permute-done.11 = bf16[8,32,768]{2,1,0:T(8,128)(2,1)} collective-permute-done((bf16[8,32,768]{2,1,0:T(8,128)(2,1)S(1)}, bf16[8,32,768]{2,1,0:T(8,128)(2,1)}, u32[]{:S(2)}, u32[]{:S(2)}) %collective-permute-start.11) | collective-permute-done | bytes 393248 | tf_op jit(solution)/shard_map/ppermute | solution.py:34
  255.4 8.4 %collective-permute-done.5 = bf16[8,32,768]{2,1,0:T(8,128)(2,1)} collective-permute-done((bf16[8,32,768]{2,1,0:T(8,128)(2,1)S(1)}, bf16[8,32,768]{2,1,0:T(8,128)(2,1)}, u32[]{:S(2)}, u32[]{:S(2)}) %collective-permute-start.5) | collective-permute-done | bytes 393248 | tf_op jit(solution)/shard_map/ppermute | solution.py:34
  263.8 8.4 %collective-permute-done.26 = bf16[8,32,768]{2,1,0:T(8,128)(2,1)} collective-permute-done((bf16[8,32,768]{2,1,0:T(8,128)(2,1)}, bf16[8,32,768]{2,1,0:T(8,128)(2,1)}, u32[]{:S(2)}, u32[]{:S(2)}) %collective-permute-start.26) | collective-permute-done | bytes 393248 | tf_op jit(solution)/shard_map/ppermute | solution.py:34
  272.2 8.4 %collective-permute-done.19 = bf16[8,32,768]{2,1,0:T(8,128)(2,1)} collective-permute-done((bf16[8,32,768]{2,1,0:T(8,128)(2,1)}, bf16[8,32,768]{2,1,0:T(8,128)(2,1)}, u32[]{:S(2)}, u32[]{:S(2)}) %collective-permute-start.19) | collective-permute-done | bytes 393248 | tf_op jit(solution)/shard_map/ppermute | solution.py:34
  280.6 8.4 %collective-permute-done.12 = bf16[8,32,768]{2,1,0:T(8,128)(2,1)} collective-permute-done((bf16[8,32,768]{2,1,0:T(8,128)(2,1)}, bf16[8,32,768]{2,1,0:T(8,128)(2,1)}, u32[]{:S(2)}, u32[]{:S(2)}) %collective-permute-start.12) | collective-permute-done | bytes 393248 | tf_op jit(solution)/shard_map/ppermute | solution.py:34
  289.1 8.4 %collective-permute-done.6 = bf16[8,32,768]{2,1,0:T(8,128)(2,1)} collective-permute-done((bf16[8,32,768]{2,1,0:T(8,128)(2,1)}, bf16[8,32,768]{2,1,0:T(8,128)(2,1)}, u32[]{:S(2)}, u32[]{:S(2)}) %collective-permute-start.6) | collective-permute-done | bytes 393248 | tf_op jit(solution)/shard_map/ppermute | solution.py:34
  303.9 17.9 %collective-permute-done.13 = bf16[8,32,768]{2,1,0:T(8,128)(2,1)S(1)} collective-permute-done((bf16[8,32,768]{2,1,0:T(8,128)(2,1)}, bf16[8,32,768]{2,1,0:T(8,128)(2,1)S(1)}, u32[]{:S(2)}, u32[]{:S(2)}) %collective-permute-start.13) | collective-permute-done | bytes 393248 | tf_op jit(solution)/shard_map/ppermute | solution.py:34
  334.7 11.3 %copy.84 = bf16[64,32,768]{0,1,2:T(8,128)(2,1)} copy(bf16[64,32,768]{2,1,0:T(8,128)(2,1)S(1)} %get-tuple-element.10) | data formatting | bytes 6291456
  346.0 12.8 %convert_bitcast_fusion = bf16[32,64,64,12]{2,1,3,0:T(8,128)(2,1)} fusion(bf16[64,32,64,12]{0,1,3,2:T(8,128)(2,1)} %bitcast.73, bf16[1,64,64]{2,1,0:T(8,128)(2,1)S(1)} %copy-done), kind=kOutput, calls=%fused_computation.24 | convolution fusion | flops 202899456 | bytes 6299648 | tf_op jit(solution)/shard_map/pq,qmai->mapi/dot_general | solution.py:42
  358.8 9.4 %copy.74 = bf16[32,64,64,12]{1,0,3,2:T(8,128)(2,1)} copy(bf16[32,64,64,12]{2,1,3,0:T(8,128)(2,1)} %convert_bitcast_fusion) | data formatting | bytes 6291456 | tf_op jit(solution)/shard_map/convert_element_type | solution.py:44
  368.3 8.7 %reshape.91 = bf16[2048,768]{0,1:T(8,128)(2,1)S(1)} reshape(bf16[32,64,64,12]{1,0,3,2:T(8,128)(2,1)} %copy.74) | data formatting | bytes 6291456 | tf_op jit(solution)/shard_map/reshape | solution.py:45
  376.9 5.9 %fusion.25 = (bf16[64,32,768]{2,1,0:T(8,128)(2,1)}, bf16[64,32,768]{2,1,0:T(8,128)(2,1)}) fusion(s32[]{:T(128)S(6)} %select_n.34, bf16[64,32,768]{2,1,0:T(8,128)(2,1)} %copy-done.5, bf16[64,32,768]{2,1,0:T(8,128)(2,1)} %copy-done.4), kind=kLoop, calls=%fused_computation.32 | loop fusion | flops 3145728 | bytes 12582916 | tf_op jit(solution)/shard_map/jit(_roll_dynamic)/concatenate | solution.py:35
  382.8 12.2 %copy.82 = bf16[64,32,768]{0,1,2:T(8,128)(2,1)} copy(bf16[64,32,768]{2,1,0:T(8,128)(2,1)} %get-tuple-element.12) | data formatting | bytes 6291456
  395.0 12.8 %convert_bitcast_fusion.2 = bf16[32,64,64,12]{2,1,3,0:T(8,128)(2,1)} fusion(bf16[64,32,64,12]{0,1,3,2:T(8,128)(2,1)} %bitcast.74, bf16[1,64,64]{2,1,0:T(8,128)(2,1)S(1)} %copy-done), kind=kOutput, calls=%fused_computation.26 | convolution fusion | flops 202899456 | bytes 6299648 | tf_op jit(solution)/shard_map/pq,qmai->mapi/dot_general | solution.py:42
  407.8 9.8 %copy.62 = bf16[32,64,64,12]{1,0,3,2:T(8,128)(2,1)} copy(bf16[32,64,64,12]{2,1,3,0:T(8,128)(2,1)} %convert_bitcast_fusion.2) | data formatting | bytes 6291456 | tf_op jit(solution)/shard_map/convert_element_type | solution.py:44
  417.6 9.7 %reshape.87 = bf16[2048,768]{0,1:T(8,128)(2,1)} reshape(bf16[32,64,64,12]{1,0,3,2:T(8,128)(2,1)} %copy.62) | data formatting | bytes 6291456 | tf_op jit(solution)/shard_map/reshape | solution.py:45
  427.3 12.2 %copy.83 = bf16[64,32,768]{0,1,2:T(8,128)(2,1)} copy(bf16[64,32,768]{2,1,0:T(8,128)(2,1)} %get-tuple-element.11) | data formatting | bytes 6291456
  439.5 12.8 %convert_bitcast_fusion.1 = bf16[32,64,64,12]{2,1,3,0:T(8,128)(2,1)} fusion(bf16[64,32,64,12]{0,1,3,2:T(8,128)(2,1)} %bitcast.75, bf16[1,64,64]{2,1,0:T(8,128)(2,1)S(1)} %copy-done), kind=kOutput, calls=%fused_computation.25 | convolution fusion | flops 202899456 | bytes 6299648 | tf_op jit(solution)/shard_map/pq,qmai->mapi/dot_general | solution.py:42
  452.3 9.4 %copy.68 = bf16[32,64,64,12]{1,0,3,2:T(8,128)(2,1)} copy(bf16[32,64,64,12]{2,1,3,0:T(8,128)(2,1)} %convert_bitcast_fusion.1) | data formatting | bytes 6291456 | tf_op jit(solution)/shard_map/convert_element_type | solution.py:44
  461.7 9.9 %reshape.89 = bf16[2048,768]{0,1:T(8,128)(2,1)} reshape(bf16[32,64,64,12]{1,0,3,2:T(8,128)(2,1)} %copy.68) | data formatting | bytes 6291456 | tf_op jit(solution)/shard_map/reshape | solution.py:45
  471.6 12.2 %copy.81 = bf16[64,32,768]{0,1,2:T(8,128)(2,1)} copy(bf16[64,32,768]{2,1,0:T(8,128)(2,1)} %get-tuple-element.13) | data formatting | bytes 6291456
  483.8 12.8 %convert_bitcast_fusion.3 = bf16[32,64,64,12]{2,1,3,0:T(8,128)(2,1)} fusion(bf16[64,32,64,12]{0,1,3,2:T(8,128)(2,1)} %bitcast.76, bf16[1,64,64]{2,1,0:T(8,128)(2,1)S(1)} %copy-done), kind=kOutput, calls=%fused_computation.27 | convolution fusion | flops 202899456 | bytes 6299648 | tf_op jit(solution)/shard_map/pq,qmai->mapi/dot_general | solution.py:42
  496.6 9.4 %copy.56 = bf16[32,64,64,12]{1,0,3,2:T(8,128)(2,1)} copy(bf16[32,64,64,12]{2,1,3,0:T(8,128)(2,1)} %convert_bitcast_fusion.3) | data formatting | bytes 6291456 | tf_op jit(solution)/shard_map/convert_element_type | solution.py:44
  506.0 9.9 %reshape.85 = bf16[2048,768]{0,1:T(8,128)(2,1)} reshape(bf16[32,64,64,12]{1,0,3,2:T(8,128)(2,1)} %copy.56) | data formatting | bytes 6291456 | tf_op jit(solution)/shard_map/reshape | solution.py:45
  524.5 30.1 %reduce-scatter.2.cloned.1.call-done = f32[512,256]{1,0:T(8,128)} async-done(((f32[2048,256]{1,0:T(8,128)}), f32[512,256]{1,0:T(8,128)}) %reduce-scatter.2.cloned.1.call-update) | async-done | bytes 524304 | tf_op jit(solution)/shard_map/reduce_scatter | solution.py:49
  (135 shorter events, 56.0 us)
Async XLA Ops:
  6.5 339.5 %copy-start = (bf16[1,64,64]{2,1,0:T(8,128)(2,1)S(1)}, bf16[1,64,64]{2,1,0:T(8,128)(2,1)}, u32[]{:S(2)}) copy-start(bf16[1,64,64]{2,1,0:T(8,128)(2,1)} %param.9) | copy-start | bytes 24580
  6.5 548.0 %reduce-scatter.2.cloned.1.call-start = ((), (), s32[]{:S(2)}) async-start(), calls=%async_computation.1 | async-start | bytes 2621440 | tf_op jit(solution)/shard_map/reduce_scatter | solution.py:49
  78.6 24.6 %collective-permute-start = (bf16[8,32,768]{2,1,0:T(8,128)(2,1)}, bf16[8,32,768]{2,1,0:T(8,128)(2,1)}, u32[]{:S(2)}, u32[]{:S(2)}) collective-permute-start(bf16[8,32,768]{2,1,0:T(8,128)(2,1)} %copy.52), channel_id=1, source_target_pairs={{0,4},{4,8},{8,12},{12,16},{16,20},{20,24},{24,28},{28,0},{1,5},{5... | collective-permute-start | bytes 1179656 | tf_op jit(solution)/shard_map/ppermute | solution.py:34
  87.9 16.8 %collective-permute-start.21 = (bf16[8,32,768]{2,1,0:T(8,128)(2,1)S(1)}, bf16[8,32,768]{2,1,0:T(8,128)(2,1)}, u32[]{:S(2)}, u32[]{:S(2)}) collective-permute-start(bf16[8,32,768]{2,1,0:T(8,128)(2,1)S(1)} %copy.70), channel_id=1, source_target_pairs={{0,4},{4,8},{8,12},{12,16},{16,20},{20,24},{24,28},{28,0},{1,5},{5... | collective-permute-start | bytes 1179656 | tf_op jit(solution)/shard_map/ppermute | solution.py:34
  95.4 16.7 %collective-permute-start.14 = (bf16[8,32,768]{2,1,0:T(8,128)(2,1)S(1)}, bf16[8,32,768]{2,1,0:T(8,128)(2,1)}, u32[]{:S(2)}, u32[]{:S(2)}) collective-permute-start(bf16[8,32,768]{2,1,0:T(8,128)(2,1)S(1)} %copy.64), channel_id=1, source_target_pairs={{0,4},{4,8},{8,12},{12,16},{16,20},{20,24},{24,28},{28,0},{1,5},{5... | collective-permute-start | bytes 1179656 | tf_op jit(solution)/shard_map/ppermute | solution.py:34
  101.6 18.8 %collective-permute-start.7 = (bf16[8,32,768]{2,1,0:T(8,128)(2,1)S(1)}, bf16[8,32,768]{2,1,0:T(8,128)(2,1)S(1)}, u32[]{:S(2)}, u32[]{:S(2)}) collective-permute-start(bf16[8,32,768]{2,1,0:T(8,128)(2,1)S(1)} %copy.58), channel_id=1, source_target_pairs={{0,4},{4,8},{8,12},{12,16},{16,20},{20,24},{24,28},{28,0},{1,5},{5... | collective-permute-start | bytes 1179656 | tf_op jit(solution)/shard_map/ppermute | solution.py:34
  103.2 25.6 %collective-permute-start.1 = (bf16[8,32,768]{2,1,0:T(8,128)(2,1)}, bf16[8,32,768]{2,1,0:T(8,128)(2,1)S(1)}, u32[]{:S(2)}, u32[]{:S(2)}) collective-permute-start(bf16[8,32,768]{2,1,0:T(8,128)(2,1)} %collective-permute-done), channel_id=1, source_target_pairs={{0,4},{4,8},{8,12},{12,16},{16,20},{20,24},{24,28},{28,0},{1,5},{5... | collective-permute-start | bytes 1179656 | tf_op jit(solution)/shard_map/ppermute | solution.py:34
  104.7 32.6 %collective-permute-start.22 = (bf16[8,32,768]{2,1,0:T(8,128)(2,1)}, bf16[8,32,768]{2,1,0:T(8,128)(2,1)S(1)}, u32[]{:S(2)}, u32[]{:S(2)}) collective-permute-start(bf16[8,32,768]{2,1,0:T(8,128)(2,1)} %collective-permute-done.21), channel_id=1, source_target_pairs={{0,4},{4,8},{8,12},{12,16},{16,20},{20,24},{24,28},{28,0},{1,5},{5... | collective-permute-start | bytes 1179656 | tf_op jit(solution)/shard_map/ppermute | solution.py:34
  112.1 33.6 %collective-permute-start.15 = (bf16[8,32,768]{2,1,0:T(8,128)(2,1)}, bf16[8,32,768]{2,1,0:T(8,128)(2,1)S(1)}, u32[]{:S(2)}, u32[]{:S(2)}) collective-permute-start(bf16[8,32,768]{2,1,0:T(8,128)(2,1)} %collective-permute-done.14), channel_id=1, source_target_pairs={{0,4},{4,8},{8,12},{12,16},{16,20},{20,24},{24,28},{28,0},{1,5},{5... | collective-permute-start | bytes 1179656 | tf_op jit(solution)/shard_map/ppermute | solution.py:34
  120.4 33.7 %collective-permute-start.8 = (bf16[8,32,768]{2,1,0:T(8,128)(2,1)S(1)}, bf16[8,32,768]{2,1,0:T(8,128)(2,1)S(1)}, u32[]{:S(2)}, u32[]{:S(2)}) collective-permute-start(bf16[8,32,768]{2,1,0:T(8,128)(2,1)S(1)} %collective-permute-done.7), channel_id=1, source_target_pairs={{0,4},{4,8},{8,12},{12,16},{16,20},{20,24},{24,28},{28,0},{1,5},{5... | collective-permute-start | bytes 1179656 | tf_op jit(solution)/shard_map/ppermute | solution.py:34
  128.8 33.7 %copy-start.10 = (bf16[8,32,768]{2,1,0:T(8,128)(2,1)}, bf16[8,32,768]{2,1,0:T(8,128)(2,1)S(1)}, u32[]{:S(2)}) copy-start(bf16[8,32,768]{2,1,0:T(8,128)(2,1)S(1)} %collective-permute-done.1) | copy-start | bytes 1179652
  128.8 33.7 %collective-permute-start.2 = (bf16[8,32,768]{2,1,0:T(8,128)(2,1)S(1)}, bf16[8,32,768]{2,1,0:T(8,128)(2,1)S(1)}, u32[]{:S(2)}, u32[]{:S(2)}) collective-permute-start(bf16[8,32,768]{2,1,0:T(8,128)(2,1)S(1)} %collective-permute-done.1), channel_id=1, source_target_pairs={{0,4},{4,8},{8,12},{12,16},{16,20},{20,24},{24,28},{28,0},{1,5},{5... | collective-permute-start | bytes 1179656 | tf_op jit(solution)/shard_map/ppermute | solution.py:34
  137.3 33.7 %collective-permute-start.23 = (bf16[8,32,768]{2,1,0:T(8,128)(2,1)S(1)}, bf16[8,32,768]{2,1,0:T(8,128)(2,1)S(1)}, u32[]{:S(2)}, u32[]{:S(2)}) collective-permute-start(bf16[8,32,768]{2,1,0:T(8,128)(2,1)S(1)} %collective-permute-done.22), channel_id=1, source_target_pairs={{0,4},{4,8},{8,12},{12,16},{16,20},{20,24},{24,28},{28,0},{1,5},{5... | collective-permute-start | bytes 1179656 | tf_op jit(solution)/shard_map/ppermute | solution.py:34
  145.7 33.7 %collective-permute-start.16 = (bf16[8,32,768]{2,1,0:T(8,128)(2,1)S(1)}, bf16[8,32,768]{2,1,0:T(8,128)(2,1)S(1)}, u32[]{:S(2)}, u32[]{:S(2)}) collective-permute-start(bf16[8,32,768]{2,1,0:T(8,128)(2,1)S(1)} %collective-permute-done.15), channel_id=1, source_target_pairs={{0,4},{4,8},{8,12},{12,16},{16,20},{20,24},{24,28},{28,0},{1,5},{5... | collective-permute-start | bytes 1179656 | tf_op jit(solution)/shard_map/ppermute | solution.py:34
  154.1 84.4 %copy-start.8 = (bf16[8,32,768]{2,1,0:T(8,128)(2,1)}, bf16[8,32,768]{2,1,0:T(8,128)(2,1)S(1)}, u32[]{:S(2)}) copy-start(bf16[8,32,768]{2,1,0:T(8,128)(2,1)S(1)} %collective-permute-done.8) | copy-start | bytes 1179652
  154.1 33.7 %collective-permute-start.9 = (bf16[8,32,768]{2,1,0:T(8,128)(2,1)S(1)}, bf16[8,32,768]{2,1,0:T(8,128)(2,1)S(1)}, u32[]{:S(2)}, u32[]{:S(2)}) collective-permute-start(bf16[8,32,768]{2,1,0:T(8,128)(2,1)S(1)} %collective-permute-done.8), channel_id=1, source_target_pairs={{0,4},{4,8},{8,12},{12,16},{16,20},{20,24},{24,28},{28,0},{1,5},{5... | collective-permute-start | bytes 1179656 | tf_op jit(solution)/shard_map/ppermute | solution.py:34
  162.6 92.8 %copy-start.16 = (bf16[8,32,768]{2,1,0:T(8,128)(2,1)}, bf16[8,32,768]{2,1,0:T(8,128)(2,1)S(1)}, u32[]{:S(2)}) copy-start(bf16[8,32,768]{2,1,0:T(8,128)(2,1)S(1)} %collective-permute-done.2) | copy-start | bytes 1179652
  162.6 33.7 %collective-permute-start.3 = (bf16[8,32,768]{2,1,0:T(8,128)(2,1)S(1)}, bf16[8,32,768]{2,1,0:T(8,128)(2,1)S(1)}, u32[]{:S(2)}, u32[]{:S(2)}) collective-permute-start(bf16[8,32,768]{2,1,0:T(8,128)(2,1)S(1)} %collective-permute-done.2), channel_id=1, source_target_pairs={{0,4},{4,8},{8,12},{12,16},{16,20},{20,24},{24,28},{28,0},{1,5},{5... | collective-permute-start | bytes 1179656 | tf_op jit(solution)/shard_map/ppermute | solution.py:34
  171.0 33.7 %collective-permute-start.24 = (bf16[8,32,768]{2,1,0:T(8,128)(2,1)S(1)}, bf16[8,32,768]{2,1,0:T(8,128)(2,1)S(1)}, u32[]{:S(2)}, u32[]{:S(2)}) collective-permute-start(bf16[8,32,768]{2,1,0:T(8,128)(2,1)S(1)} %collective-permute-done.23), channel_id=1, source_target_pairs={{0,4},{4,8},{8,12},{12,16},{16,20},{20,24},{24,28},{28,0},{1,5},{5... | collective-permute-start | bytes 1179656 | tf_op jit(solution)/shard_map/ppermute | solution.py:34
  179.4 59.1 %copy-start.6 = (bf16[8,32,768]{2,1,0:T(8,128)(2,1)}, bf16[8,32,768]{2,1,0:T(8,128)(2,1)S(1)}, u32[]{:S(2)}) copy-start(bf16[8,32,768]{2,1,0:T(8,128)(2,1)S(1)} %collective-permute-done.16) | copy-start | bytes 1179652
  179.4 33.7 %collective-permute-start.17 = (bf16[8,32,768]{2,1,0:T(8,128)(2,1)S(1)}, bf16[8,32,768]{2,1,0:T(8,128)(2,1)S(1)}, u32[]{:S(2)}, u32[]{:S(2)}) collective-permute-start(bf16[8,32,768]{2,1,0:T(8,128)(2,1)S(1)} %collective-permute-done.16), channel_id=1, source_target_pairs={{0,4},{4,8},{8,12},{12,16},{16,20},{20,24},{24,28},{28,0},{1,5},{5... | collective-permute-start | bytes 1179656 | tf_op jit(solution)/shard_map/ppermute | solution.py:34
  187.8 59.1 %copy-start.14 = (bf16[8,32,768]{2,1,0:T(8,128)(2,1)}, bf16[8,32,768]{2,1,0:T(8,128)(2,1)S(1)}, u32[]{:S(2)}) copy-start(bf16[8,32,768]{2,1,0:T(8,128)(2,1)S(1)} %collective-permute-done.9) | copy-start | bytes 1179652
  187.8 33.7 %collective-permute-start.10 = (bf16[8,32,768]{2,1,0:T(8,128)(2,1)S(1)}, bf16[8,32,768]{2,1,0:T(8,128)(2,1)S(1)}, u32[]{:S(2)}, u32[]{:S(2)}) collective-permute-start(bf16[8,32,768]{2,1,0:T(8,128)(2,1)S(1)} %collective-permute-done.9), channel_id=1, source_target_pairs={{0,4},{4,8},{8,12},{12,16},{16,20},{20,24},{24,28},{28,0},{1,5},{5... | collective-permute-start | bytes 1179656 | tf_op jit(solution)/shard_map/ppermute | solution.py:34
  196.3 67.5 %copy-start.20 = (bf16[8,32,768]{2,1,0:T(8,128)(2,1)}, bf16[8,32,768]{2,1,0:T(8,128)(2,1)S(1)}, u32[]{:S(2)}) copy-start(bf16[8,32,768]{2,1,0:T(8,128)(2,1)S(1)} %collective-permute-done.3) | copy-start | bytes 1179652
  196.3 33.7 %collective-permute-start.4 = (bf16[8,32,768]{2,1,0:T(8,128)(2,1)S(1)}, bf16[8,32,768]{2,1,0:T(8,128)(2,1)S(1)}, u32[]{:S(2)}, u32[]{:S(2)}) collective-permute-start(bf16[8,32,768]{2,1,0:T(8,128)(2,1)S(1)} %collective-permute-done.3), channel_id=1, source_target_pairs={{0,4},{4,8},{8,12},{12,16},{16,20},{20,24},{24,28},{28,0},{1,5},{5... | collective-permute-start | bytes 1179656 | tf_op jit(solution)/shard_map/ppermute | solution.py:34
  204.7 33.8 %collective-permute-start.25 = (bf16[8,32,768]{2,1,0:T(8,128)(2,1)S(1)}, bf16[8,32,768]{2,1,0:T(8,128)(2,1)}, u32[]{:S(2)}, u32[]{:S(2)}) collective-permute-start(bf16[8,32,768]{2,1,0:T(8,128)(2,1)S(1)} %collective-permute-done.24), channel_id=1, source_target_pairs={{0,4},{4,8},{8,12},{12,16},{16,20},{20,24},{24,28},{28,0},{1,5},{5... | collective-permute-start | bytes 1179656 | tf_op jit(solution)/shard_map/ppermute | solution.py:34
  213.1 33.8 %copy-start.12 = (bf16[8,32,768]{2,1,0:T(8,128)(2,1)}, bf16[8,32,768]{2,1,0:T(8,128)(2,1)S(1)}, u32[]{:S(2)}) copy-start(bf16[8,32,768]{2,1,0:T(8,128)(2,1)S(1)} %collective-permute-done.17) | copy-start | bytes 1179652
  213.1 33.8 %collective-permute-start.18 = (bf16[8,32,768]{2,1,0:T(8,128)(2,1)S(1)}, bf16[8,32,768]{2,1,0:T(8,128)(2,1)}, u32[]{:S(2)}, u32[]{:S(2)}) collective-permute-start(bf16[8,32,768]{2,1,0:T(8,128)(2,1)S(1)} %collective-permute-done.17), channel_id=1, source_target_pairs={{0,4},{4,8},{8,12},{12,16},{16,20},{20,24},{24,28},{28,0},{1,5},{5... | collective-permute-start | bytes 1179656 | tf_op jit(solution)/shard_map/ppermute | solution.py:34
  221.5 33.8 %copy-start.18 = (bf16[8,32,768]{2,1,0:T(8,128)(2,1)}, bf16[8,32,768]{2,1,0:T(8,128)(2,1)S(1)}, u32[]{:S(2)}) copy-start(bf16[8,32,768]{2,1,0:T(8,128)(2,1)S(1)} %collective-permute-done.10) | copy-start | bytes 1179652
  221.5 33.8 %collective-permute-start.11 = (bf16[8,32,768]{2,1,0:T(8,128)(2,1)S(1)}, bf16[8,32,768]{2,1,0:T(8,128)(2,1)}, u32[]{:S(2)}, u32[]{:S(2)}) collective-permute-start(bf16[8,32,768]{2,1,0:T(8,128)(2,1)S(1)} %collective-permute-done.10), channel_id=1, source_target_pairs={{0,4},{4,8},{8,12},{12,16},{16,20},{20,24},{24,28},{28,0},{1,5},{5... | collective-permute-start | bytes 1179656 | tf_op jit(solution)/shard_map/ppermute | solution.py:34
  230.0 33.8 %copy-start.21 = (bf16[8,32,768]{2,1,0:T(8,128)(2,1)}, bf16[8,32,768]{2,1,0:T(8,128)(2,1)S(1)}, u32[]{:S(2)}) copy-start(bf16[8,32,768]{2,1,0:T(8,128)(2,1)S(1)} %collective-permute-done.4) | copy-start | bytes 1179652
  230.0 33.8 %collective-permute-start.5 = (bf16[8,32,768]{2,1,0:T(8,128)(2,1)S(1)}, bf16[8,32,768]{2,1,0:T(8,128)(2,1)}, u32[]{:S(2)}, u32[]{:S(2)}) collective-permute-start(bf16[8,32,768]{2,1,0:T(8,128)(2,1)S(1)} %collective-permute-done.4), channel_id=1, source_target_pairs={{0,4},{4,8},{8,12},{12,16},{16,20},{20,24},{24,28},{28,0},{1,5},{5... | collective-permute-start | bytes 1179656 | tf_op jit(solution)/shard_map/ppermute | solution.py:34
  238.5 33.7 %collective-permute-start.26 = (bf16[8,32,768]{2,1,0:T(8,128)(2,1)}, bf16[8,32,768]{2,1,0:T(8,128)(2,1)}, u32[]{:S(2)}, u32[]{:S(2)}) collective-permute-start(bf16[8,32,768]{2,1,0:T(8,128)(2,1)} %collective-permute-done.25), channel_id=1, source_target_pairs={{0,4},{4,8},{8,12},{12,16},{16,20},{20,24},{24,28},{28,0},{1,5},{5... | collective-permute-start | bytes 1179656 | tf_op jit(solution)/shard_map/ppermute | solution.py:34
  246.9 33.7 %collective-permute-start.19 = (bf16[8,32,768]{2,1,0:T(8,128)(2,1)}, bf16[8,32,768]{2,1,0:T(8,128)(2,1)}, u32[]{:S(2)}, u32[]{:S(2)}) collective-permute-start(bf16[8,32,768]{2,1,0:T(8,128)(2,1)} %collective-permute-done.18), channel_id=1, source_target_pairs={{0,4},{4,8},{8,12},{12,16},{16,20},{20,24},{24,28},{28,0},{1,5},{5... | collective-permute-start | bytes 1179656 | tf_op jit(solution)/shard_map/ppermute | solution.py:34
  255.4 33.7 %collective-permute-start.12 = (bf16[8,32,768]{2,1,0:T(8,128)(2,1)}, bf16[8,32,768]{2,1,0:T(8,128)(2,1)}, u32[]{:S(2)}, u32[]{:S(2)}) collective-permute-start(bf16[8,32,768]{2,1,0:T(8,128)(2,1)} %collective-permute-done.11), channel_id=1, source_target_pairs={{0,4},{4,8},{8,12},{12,16},{16,20},{20,24},{24,28},{28,0},{1,5},{5... | collective-permute-start | bytes 1179656 | tf_op jit(solution)/shard_map/ppermute | solution.py:34
  263.8 33.7 %collective-permute-start.6 = (bf16[8,32,768]{2,1,0:T(8,128)(2,1)}, bf16[8,32,768]{2,1,0:T(8,128)(2,1)}, u32[]{:S(2)}, u32[]{:S(2)}) collective-permute-start(bf16[8,32,768]{2,1,0:T(8,128)(2,1)} %collective-permute-done.5), channel_id=1, source_target_pairs={{0,4},{4,8},{8,12},{12,16},{16,20},{20,24},{24,28},{28,0},{1,5},{5... | collective-permute-start | bytes 1179656 | tf_op jit(solution)/shard_map/ppermute | solution.py:34
  263.8 37.8 %copy-start.17 = (bf16[8,32,768]{2,1,0:T(8,128)(2,1)S(1)}, bf16[8,32,768]{2,1,0:T(8,128)(2,1)}, u32[]{:S(2)}) copy-start(bf16[8,32,768]{2,1,0:T(8,128)(2,1)} %copy-done.16) | copy-start | bytes 1179652
  263.8 37.9 %copy-start.11 = (bf16[8,32,768]{2,1,0:T(8,128)(2,1)S(1)}, bf16[8,32,768]{2,1,0:T(8,128)(2,1)}, u32[]{:S(2)}) copy-start(bf16[8,32,768]{2,1,0:T(8,128)(2,1)} %copy-done.10) | copy-start | bytes 1179652
  272.2 55.6 %collective-permute-start.27 = (bf16[8,32,768]{2,1,0:T(8,128)(2,1)}, bf16[8,32,768]{2,1,0:T(8,128)(2,1)S(1)}, u32[]{:S(2)}, u32[]{:S(2)}) collective-permute-start(bf16[8,32,768]{2,1,0:T(8,128)(2,1)} %collective-permute-done.26), channel_id=1, source_target_pairs={{0,4},{4,8},{8,12},{12,16},{16,20},{20,24},{24,28},{28,0},{1,5},{5... | collective-permute-start | bytes 1179656 | tf_op jit(solution)/shard_map/ppermute | solution.py:34
  280.6 43.5 %collective-permute-start.20 = (bf16[8,32,768]{2,1,0:T(8,128)(2,1)}, bf16[8,32,768]{2,1,0:T(8,128)(2,1)S(1)}, u32[]{:S(2)}, u32[]{:S(2)}) collective-permute-start(bf16[8,32,768]{2,1,0:T(8,128)(2,1)} %collective-permute-done.19), channel_id=1, source_target_pairs={{0,4},{4,8},{8,12},{12,16},{16,20},{20,24},{24,28},{28,0},{1,5},{5... | collective-permute-start | bytes 1179656 | tf_op jit(solution)/shard_map/ppermute | solution.py:34
  289.1 32.8 %collective-permute-start.13 = (bf16[8,32,768]{2,1,0:T(8,128)(2,1)}, bf16[8,32,768]{2,1,0:T(8,128)(2,1)S(1)}, u32[]{:S(2)}, u32[]{:S(2)}) collective-permute-start(bf16[8,32,768]{2,1,0:T(8,128)(2,1)} %collective-permute-done.12), channel_id=1, source_target_pairs={{0,4},{4,8},{8,12},{12,16},{16,20},{20,24},{24,28},{28,0},{1,5},{5... | collective-permute-start | bytes 1179656 | tf_op jit(solution)/shard_map/ppermute | solution.py:34
  300.6 23.4 %copy-start.19 = (bf16[8,32,768]{2,1,0:T(8,128)(2,1)S(1)}, bf16[8,32,768]{2,1,0:T(8,128)(2,1)}, u32[]{:S(2)}) copy-start(bf16[8,32,768]{2,1,0:T(8,128)(2,1)} %copy-done.18) | copy-start | bytes 1179652
  301.7 22.3 %copy-start.15 = (bf16[8,32,768]{2,1,0:T(8,128)(2,1)S(1)}, bf16[8,32,768]{2,1,0:T(8,128)(2,1)}, u32[]{:S(2)}) copy-start(bf16[8,32,768]{2,1,0:T(8,128)(2,1)} %copy-done.14) | copy-start | bytes 1179652
  301.7 22.3 %copy-start.9 = (bf16[8,32,768]{2,1,0:T(8,128)(2,1)S(1)}, bf16[8,32,768]{2,1,0:T(8,128)(2,1)}, u32[]{:S(2)}) copy-start(bf16[8,32,768]{2,1,0:T(8,128)(2,1)} %copy-done.8) | copy-start | bytes 1179652
  303.9 20.3 %copy-start.4 = (bf16[64,32,768]{2,1,0:T(8,128)(2,1)}, bf16[64,32,768]{2,1,0:T(8,128)(2,1)S(1)}, u32[]{:S(2)}) copy-start(bf16[64,32,768]{2,1,0:T(8,128)(2,1)S(1)} %constant_dynamic-update-slice_fusion) | copy-start | bytes 9437188
  323.9 2.6 copy-start.13
  324.2 3.6 copy-start.5
  515.9 3.2 copy-start.2
  (4 other events, 8.7 us)
Sparse Core Ops, SparseCore 0:
  524.6 29.8 reduce-scatter.1
